TPU v7x, 256 devices: a whole 4x4x8 slice. The times are simulated.
256 devices in a mesh: dp: 4 (over x), seq: 4 (over y_hi, core), tensor: 16 (over y_lo, z).
Axes of the slice: x: 4, y: 4 (y_hi: 2, y_lo: 2; y = y_hi * 2 + y_lo), z: 8, core: 2. Of those that a mesh axis runs over, the one named last changes fastest.
Arguments:
- byte_acts: bfloat16 [4, 16384, 2048], P('dp', 'seq', 'tensor'), may hold values from -18 to 18
- conv_weight: bfloat16 [16, 1024, 128], P('tensor'), may hold values from -0.1875 to 0.1875
- conv_bias: float32 [2048], P('tensor'), may hold values from -3 to 3
- proj_weight: bfloat16 [2048, 8192], P(None, 'tensor'), may hold values from -0.125 to 0.125
- teacher: bfloat16 [4, 4096, 8192], P('dp', 'seq', 'tensor'), may hold values from -6 to 6
- span_lengths: int32 [4, 4096], P('dp'), may hold values from 1 to 16, as said below
Outputs:
- downsampled: bfloat16 [4, 4096, 2048], P('dp', 'seq', 'tensor')
- byte_grad: bfloat16 [4, 16384, 2048], P('dp', 'seq', 'tensor')
- conv_grad: float32 [16, 1024, 128], P('tensor')
- proj_grad: float32 [2048, 8192], P(None, 'tensor')
Inputs may be any that keep to these rules, and one draw needn't show every extreme that they name: `span_lengths`: each document's 4096 span lengths cover its 16384 bytes in order; the longest is exactly 16.
All inputs are finite; a program needn't handle non-finite values.
Results may differ from a plain program's by a relative error of at most 0.019.
Values may be sent and summed in bfloat16 or wider, within the bound.
No kernel may reach another device: no remote copies, remote signals or barrier semaphores. Data moves between devices by JAX's collectives and lax.ppermute only.
A program may use at most 64 MiB of HBM per device.

v0:
```python
import jax
import jax.numpy as jnp
from jax import lax
from jax.sharding import PartitionSpec as P

STRIDE = 4
KERNEL = 8


def shifted(block, axis, distance):
    devices = range(lax.axis_size(axis))
    route = [(i - distance, i) for i in devices if i - distance in devices]
    return lax.ppermute(block, axis, route)


def intersection_weights(span_start, span_end, span_lengths, first_position, position_count):
    byte_first = (first_position + jnp.arange(position_count, dtype=jnp.int32)) * STRIDE
    lower_edge = jnp.maximum(span_start[:, None], byte_first[None, :])
    upper_edge = jnp.minimum(span_end[:, None], byte_first[None, :] + STRIDE)
    covered = jnp.maximum(upper_edge - lower_edge, 0).astype(jnp.float32)
    return (covered / span_lengths[:, None].astype(jnp.float32)).astype(jnp.bfloat16)


def local(byte_acts, conv_weight, conv_bias, proj_weight, teacher, span_lengths):
    byte_rows = byte_acts[0]
    row_total, width = byte_rows.shape
    groups_here = conv_weight.shape[0]
    group_width = width // groups_here
    positions = row_total // STRIDE
    seq_count = lax.axis_size("seq")
    seq_rank = lax.axis_index("seq")
    lengths_doc = span_lengths[0]
    tokens_all = lengths_doc.shape[0]
    span_end = jnp.cumsum(lengths_doc)
    span_start = span_end - lengths_doc
    next_rows = shifted(byte_rows[:STRIDE], "seq", -1)
    extended = jnp.concatenate([byte_rows, next_rows], axis=0)
    blocks = extended.reshape(positions + 1, STRIDE, groups_here, group_width)
    windows = jnp.concatenate([blocks[:-1], blocks[1:]], axis=1)
    taps_weight = conv_weight.reshape(groups_here, KERNEL, group_width, group_width)
    conv_out = jnp.einsum(
        "pkgc,gkco->pgo", windows, taps_weight, preferred_element_type=jnp.float32
    )
    conv_out = conv_out + conv_bias.reshape(groups_here, group_width)[None]
    downsampled = conv_out.reshape(positions, width).astype(jnp.bfloat16)
    local_weight = intersection_weights(
        span_start, span_end, lengths_doc, seq_rank * positions, positions
    )
    weight_part = local_weight
    pooled_sum = lax.psum_scatter(
        jnp.dot(weight_part, downsampled, preferred_element_type=jnp.float32).astype(jnp.bfloat16),
        "seq",
        scatter_dimension=0,
        tiled=True,
    )
    gathered = lax.all_gather(pooled_sum, "tensor", axis=1, tiled=True)
    predicted = jnp.dot(gathered, proj_weight, preferred_element_type=jnp.float32)
    err_grad = (predicted - teacher[0].astype(jnp.float32)).astype(jnp.bfloat16)
    proj_local = lax.dot_general(
        gathered, err_grad, (((0,), (0,)), ((), ())), preferred_element_type=jnp.float32
    )
    token_scale = 1.0 / jnp.sqrt(jnp.float32(lax.axis_size("dp") * tokens_all))
    proj_summed = lax.psum(proj_local.astype(jnp.bfloat16), ("dp", "seq")).astype(jnp.float32)
    proj_grad = proj_summed * token_scale
    weight_part = proj_weight
    pooled_grad_t = lax.psum_scatter(
        lax.dot_general(
            weight_part, err_grad, (((1,), (1,)), ((), ())), preferred_element_type=jnp.float32
        ).astype(jnp.bfloat16),
        "tensor",
        scatter_dimension=0,
        tiled=True,
    )
    weight_part = local_weight
    down_sum = lax.dot_general(
        weight_part,
        lax.all_gather(pooled_grad_t, "seq", axis=1, tiled=True),
        (((0,), (1,)), ((), ())),
        preferred_element_type=jnp.float32,
    )
    down_grad = down_sum.astype(jnp.bfloat16).reshape(positions, groups_here, group_width)
    conv_local = jnp.einsum(
        "pkgc,pgo->gkco", windows, down_grad, preferred_element_type=jnp.float32
    )
    conv_summed = lax.psum(conv_local.astype(jnp.bfloat16), ("dp", "seq")).astype(jnp.float32)
    position_scale = 1.0 / jnp.sqrt(jnp.float32(lax.axis_size("dp") * positions * seq_count))
    conv_grad = (conv_summed * position_scale).reshape(
        groups_here, KERNEL * group_width, group_width
    )
    window_grad = jnp.einsum(
        "pgo,gkco->pkgc", down_grad, taps_weight, preferred_element_type=jnp.float32
    )
    incoming = shifted(window_grad[-1, STRIDE:], "seq", 1)
    carried_grad = jnp.concatenate([incoming[None], window_grad[:-1, STRIDE:]], axis=0)
    byte_grad = (
        (window_grad[:, :STRIDE] + carried_grad).reshape(row_total, width).astype(jnp.bfloat16)
    )
    return (downsampled[None], byte_grad[None], conv_grad, proj_grad)


def solution(mesh):
    return jax.shard_map(
        local,
        mesh=mesh,
        in_specs=(
            P("dp", "seq", "tensor"),
            P("tensor", None, None),
            P("tensor"),
            P(None, "tensor"),
            P("dp", "seq", "tensor"),
            P("dp", None),
        ),
        out_specs=(
            P("dp", "seq", "tensor"),
            P("dp", "seq", "tensor"),
            P("tensor", None, None),
            P(None, "tensor"),
        ),
        check_vma=False,
    )
```

profile of v0, /device:TPU:1, one launch (start us, length us, event | category | flops | bytes accessed | tf_op | source)
XLA Modules:
  0.0 448.6 jit_solution(9548664783384587583)
XLA Ops:
  7.2 0.8 slice_bitcast_fusion
  8.1 5.1 %collective-permute-start = (bf16[4,128]{1,0:T(4,128)(2,1)S(1)}, bf16[4,128]{1,0:T(4,128)(2,1)S(1)}, u32[]{:S(2)}, u32[]{:S(2)}) collective-permute-start(bf16[4,128]{1,0:T(4,128)(2,1)S(1)} %slice_bitcast_fusion), channel_id=1, source_target_pairs={{16,0},{32,16},{48,32},{17,1},{33,17},{49,33},{18,2},{34,18},{50,3... | collective-permute-start | bytes 3080 | tf_op jit(solution)/shard_map/ppermute | solution.py:13
  13.2 1.0 reduce-window.9
  14.5 0.8 fusion.23
  15.3 0.7 convert_element_type.87
  16.0 1.4 copy.17
  17.4 1.5 pad_maximum_fusion
  19.1 1.0 copy-done.1
  20.0 0.7 fusion.11
  20.8 0.7 copy-done.7
  21.5 7.5 %fusion.2 = bf16[4096,128]{1,0:T(8,128)(2,1)} fusion(f32[4096]{0:T(1024)S(1)} %convert_element_type.87, s32[1024]{0:T(1024)S(1)} %add_multiply_fusion, s32[4096]{0:T(1024)S(1)} %get-tuple-element.6, s32[1024]{0:T(1024)S(1)} %broadcast_add_fusion, s32[4096]{0:T(1024)S(1)} %get-tuple-element.7, bf16[1,128,1024]{1,2,0:T(8,128)(2,1)S(1)} %fusion.11), kind=kOutput, calls=%fused_computation.3 | convolution fusion | flops 1103626240 | bytes 1368064 | tf_op jit(solution)/shard_map/dot_general | solution.py:51
  29.0 38.1 %reduce-scatter.5.cloned.1.call-done = bf16[1024,128]{1,0:T(8,128)(2,1)} async-done(((bf16[4096,128]{1,0:T(8,128)(2,1)}), bf16[1024,128]{1,0:T(8,128)(2,1)}) %reduce-scatter.5.cloned.1.call-update) | async-done | bytes 262160 | tf_op jit(solution)/shard_map/reduce_scatter | solution.py:50
  67.2 80.8 %all-gather.3.cloned.1.call-done = bf16[1024,2048]{1,0:T(8,128)(2,1)} async-done(((bf16[1024,128]{1,0:T(8,128)(2,1)}), bf16[1024,2048]{1,0:T(8,128)(2,1)}) %all-gather.3.cloned.1.call-update) | async-done | bytes 4194320 | tf_op jit(solution)/shard_map/all_gather | solution.py:56
  148.1 4.6 %fusion.24 = f32[1024,512]{1,0:T(8,128)S(1)} fusion(bf16[1024,2048]{1,0:T(8,128)(2,1)} %all-gather.3.cloned.1.call-done, bf16[2048,512]{1,0:T(8,128)(2,1)S(1)} %copy-done), kind=kOutput, calls=%fused_computation.37 | convolution fusion | flops 2147483648 | bytes 8388608 | tf_op jit(solution)/shard_map/dot_general | solution.py:57
  152.7 1.4 copy-done.8
  154.0 4.4 convert_bitcast_fusion
  158.4 6.4 %copy.23 = bf16[2048,1024]{1,0:T(8,128)(2,1)} copy(bf16[2048,1024]{0,1:T(8,128)(2,1)} %convert_bitcast_fusion) | data formatting | bytes 8388608
  164.9 78.6 %reduce-scatter.7.cloned.1.call-done = bf16[128,1024]{1,0:T(8,128)(2,1)} async-done(((bf16[2048,1024]{1,0:T(8,128)(2,1)}), bf16[128,1024]{1,0:T(8,128)(2,1)}) %reduce-scatter.7.cloned.1.call-update) | async-done | bytes 262160
  243.5 1.8 copy.24
  245.6 6.8 %convolution_convert_fusion = bf16[2048,512]{1,0:T(8,128)(2,1)} fusion(bf16[1024,2048]{1,0:T(8,128)(2,1)} %all-gather.3.cloned.1.call-done, f32[1024,512]{1,0:T(8,128)} %copy-done.8, bf16[1,1024,512]{2,1,0:T(8,128)(2,1)} %param.10), kind=kOutput, calls=%fused_computation.6 | convolution fusion | flops 2150105088 | bytes 9437184 | tf_op jit(solution)/shard_map/dot_general | solution.py:59
  252.3 24.2 %all-gather.5.cloned.1.call-done = bf16[128,4096]{0,1:T(8,128)(2,1)} async-done(((bf16[128,1024]{0,1:T(8,128)(2,1)}), bf16[128,4096]{0,1:T(8,128)(2,1)}) %all-gather.5.cloned.1.call-update) | async-done | bytes 1048592 | tf_op jit(solution)/shard_map/all_gather | solution.py:77
  276.5 7.7 %fusion.15 = bf16[1024,128,1]{1,0,2:T(8,128)(2,1)S(1)} fusion(bf16[128,4096]{0,1:T(8,128)(2,1)} %all-gather.5.cloned.1.call-done, f32[4096]{0:T(1024)S(1)} %convert_element_type.87, s32[1024]{0:T(1024)S(1)} %add_multiply_fusion, s32[4096]{0:T(1024)S(1)} %get-tuple-element.6, s32[1024]{0:T(1024)S(1)} %broadcast_add_fusion, s32[4096]{0:T(1024)S(1)} %get-tuple-element.7), kind=kOutput, calls=%fused_computation.21 | convolution fusion | flops 1103233024 | bytes 1368064 | tf_op jit(solution)/shard_map/dot_general | solution.py:75
  284.2 0.7 copy-done.4
  284.9 1.4 fusion.14
  286.4 1.7 convolution_bitcast_fusion
  288.1 2.1 collective-permute-start.1
  290.3 0.8 collective-permute-done.1
  291.1 0.3 fusion.3
  291.4 1.8 copy.20
  293.2 142.9 %all-reduce.3.cloned.1.call-done = (bf16[1,8,128,128]{3,2,1,0:T(8,128)(2,1)}, bf16[2048,512]{1,0:T(8,128)(2,1)}) async-done(((bf16[1,8,128,128]{3,2,1,0:T(8,128)(2,1)}, bf16[2048,512]{1,0:T(8,128)(2,1)}), (bf16[1,8,128,128]{3,2,1,0:T(8,128)(2,1)}, bf16[2048,512]{1,0:T(8,128)(2,1)})) %all-reduce.3.cloned.1.call-update) | async-done | bytes 2359312 | tf_op jit(solution)/shard_map/psum | solution.py:85
  436.1 1.8 convert_multiply_fusion.1
  437.9 4.2 convert_multiply_fusion
  (33 shorter events, 1.0 us)
Async XLA Ops:
  7.2 140.9 %copy-start = (bf16[2048,512]{1,0:T(8,128)(2,1)S(1)}, bf16[2048,512]{1,0:T(8,128)(2,1)}, u32[]{:S(2)}) copy-start(bf16[2048,512]{1,0:T(8,128)(2,1)} %param.9) | copy-start | bytes 6291460
  7.2 12.8 %copy-start.6 = (f32[128]{0:T(128)S(1)}, f32[128]{0:T(128)}, u32[]{:S(2)}) copy-start(f32[128]{0:T(128)} %param.8) | copy-start | bytes 1540
  7.2 12.8 %copy-start.3 = (bf16[1,1024,128]{2,1,0:T(8,128)(2,1)S(1)}, bf16[1,1024,128]{2,1,0:T(8,128)(2,1)}, u32[]{:S(2)}) copy-start(bf16[1,1024,128]{2,1,0:T(8,128)(2,1)} %param.7) | copy-start | bytes 786436
  7.2 60.0 %reduce-scatter.5.cloned.1.call-start = ((), (), s32[]{:S(2)}) async-start(), calls=%async_computation.2 | async-start | bytes 1310720 | tf_op jit(solution)/shard_map/reduce_scatter | solution.py:50
  8.1 9.3 %collective-permute-start = (bf16[4,128]{1,0:T(4,128)(2,1)S(1)}, bf16[4,128]{1,0:T(4,128)(2,1)S(1)}, u32[]{:S(2)}, u32[]{:S(2)}) collective-permute-start(bf16[4,128]{1,0:T(4,128)(2,1)S(1)} %slice_bitcast_fusion), channel_id=1, source_target_pairs={{16,0},{32,16},{48,32},{17,1},{33,17},{49,33},{18,2},{34,18},{50,3... | collective-permute-start | bytes 3080 | tf_op jit(solution)/shard_map/ppermute | solution.py:13
  19.0 1.0 copy-start.1
  20.7 0.7 copy-start.7
  29.0 119.1 %all-gather.3.cloned.1.call-start = ((), (), s32[]{:S(2)}) async-start(), calls=%async_computation.3 | async-start | bytes 4456448 | tf_op jit(solution)/shard_map/all_gather | solution.py:56
  67.2 176.3 %reduce-scatter.7.cloned.1.call-start = ((), (), s32[]{:S(2)}) async-start(), calls=%async_computation.5 | async-start | bytes 4456448
  148.1 6.0 %copy-start.5 = (bf16[1,1024,512]{2,1,0:T(8,128)(2,1)S(1)}, bf16[1,1024,512]{2,1,0:T(8,128)(2,1)}, u32[]{:S(2)}) copy-start(bf16[1,1024,512]{2,1,0:T(8,128)(2,1)} %param.10) | copy-start | bytes 3145732
  152.7 1.4 copy-start.8
  164.9 111.6 %all-gather.5.cloned.1.call-start = ((), (), s32[]{:S(2)}) async-start(), calls=%async_computation.4 | async-start | bytes 1310720 | tf_op jit(solution)/shard_map/all_gather | solution.py:77
  245.3 190.8 %all-reduce.3.cloned.1.call-start = ((), (), s32[]{:S(2)}) async-start(), calls=%async_computation.6 | async-start | bytes 4718592 | tf_op jit(solution)/shard_map/psum | solution.py:85
  276.5 8.4 %copy-start.2 = (bf16[1024,4,1,128]{3,0,1,2:T(8,128)(2,1)S(1)}, bf16[1024,4,1,128]{3,0,1,2:T(8,128)(2,1)}, u32[]{:S(2)}) copy-start(bf16[1024,4,1,128]{3,0,1,2:T(8,128)(2,1)} %copy-done.1) | copy-start | bytes 3145732
  284.2 0.7 copy-start.4
  288.1 3.1 collective-permute-start.1
Sparse Core Ops, SparseCore 0:
  29.1 38.0 reduce-scatter.4
  69.0 79.0 all-gather.2
  165.0 78.4 reduce-scatter.6
  245.9 30.5 all-gather.4
  286.5 149.5 all-reduce.2
where the time goes:
time: 449 us
  waiting for transfers between devices  366 us (82%)
  matrix products  34.8 us (8%)
  local copies, waits for them, and re-layouts  16.4 us (4%)
  between operations  13.9 us (3%)
  other arithmetic  10.3 us (2%)
  starting transfers between devices  7.58 us (2%)
    psum x1, waiting for transfers between devices, local(): lax.psum(conv_local.astype(jnp.bfloat16), ('dp', 'seq')).astype(jnp.float32)  143 us
    all_gather x1, waiting for transfers between devices, local(): gathered = lax.all_gather(pooled_sum, 'tensor', axis=1, tiled=True)  80.8 us
    unnamed x6, waiting for transfers between devices  78.7 us
    reduce_scatter x1, waiting for transfers between devices, local(): lax.psum_scatter(jnp.dot(weight_part, downsampled, preferred_element_type...  38.1 us
    all_gather x1, waiting for transfers between devices, local(): lax.all_gather(pooled_grad_t, 'seq', axis=1, tiled=True)  24.2 us
    unnamed x20, local copies, waits for them, and re-layouts  12 us
  transfers between devices with their start and end apart: 7, of which 6 were waited for; matrix products, arithmetic and copies ran while one was open for 3% of the time, Pallas kernels for 0%

commit v1 on v0

--- a/solution.py
+++ b/solution.py
@@ -82,7 +82,8 @@
     conv_local = jnp.einsum(
         "pkgc,pgo->gkco", windows, down_grad, preferred_element_type=jnp.float32
     )
-    conv_summed = lax.psum(conv_local.astype(jnp.bfloat16), ("dp", "seq")).astype(jnp.float32)
+    advance_heaps_up = lambda frame_in: lax.psum(lax.psum(frame_in, "seq"), "dp")
+    conv_summed = advance_heaps_up(conv_local.astype(jnp.bfloat16)).astype(jnp.float32)
     position_scale = 1.0 / jnp.sqrt(jnp.float32(lax.axis_size("dp") * positions * seq_count))
     conv_grad = (conv_summed * position_scale).reshape(
         groups_here, KERNEL * group_width, group_width

time: 449 us -> 536 us (1.19)
  waiting for transfers between devices: 366 us -> 447 us
    psum x1 -> x3, waiting for transfers between devices: 143 us -> 224 us  [the longest x1 138 us: local(): lax.psum(proj_local.astype(jnp.bfloat16), ('dp', 'seq')).astype(jnp.float32)]
    unnamed x20 -> x22, local copies, waits for them, and re-layouts: 12 us -> 13.2 us
    unnamed x6 -> x8, waiting for transfers between devices: 78.7 us -> 78.6 us
  transfers between devices with their start and end apart: 7 -> 9, of which waited for: 6 -> 7; matrix products, arithmetic and copies ran while one was open for 3% -> 6% of each run, Pallas kernels for 0% -> 0%
where the time goes in v1:
time: 536 us; the launch traced here: 534 us
  waiting for transfers between devices  447 us (83%)
  matrix products  33.7 us (6%)
  local copies, waits for them, and re-layouts  19 us (4%)
  between operations  14.3 us (3%)
  other arithmetic  12.7 us (2%)
  starting transfers between devices  7.66 us (1%)
    psum x1, waiting for transfers between devices, local(): lax.psum(proj_local.astype(jnp.bfloat16), ('dp', 'seq')).astype(jnp.float32)  138 us
    all_gather x1, waiting for transfers between devices, local(): gathered = lax.all_gather(pooled_sum, 'tensor', axis=1, tiled=True)  80.8 us
    unnamed x8, waiting for transfers between devices  78.6 us
    psum x1, waiting for transfers between devices, local(): lax.psum(frame_in, 'seq')  45.1 us
    psum x1, waiting for transfers between devices, local(): lax.psum(lax.psum(frame_in, 'seq'), 'dp')  41.6 us
    reduce_scatter x1, waiting for transfers between devices, local(): lax.psum_scatter(jnp.dot(weight_part, downsampled, preferred_element_type...  38.1 us
    all_gather x1, waiting for transfers between devices, local(): lax.all_gather(pooled_grad_t, 'seq', axis=1, tiled=True)  24.6 us
    unnamed x22, local copies, waits for them, and re-layouts  13.2 us
  transfers between devices with their start and end apart: 9, of which 7 were waited for; matrix products, arithmetic and copies ran while one was open for 6% of the time, Pallas kernels for 0%

profile of v1, /device:TPU:1, one launch (start us, length us, event | category | flops | bytes accessed | tf_op | source)
XLA Modules:
  0.0 533.9 jit_solution(10340372007217103008)
XLA Ops:
  7.2 0.8 slice_bitcast_fusion
  8.1 5.1 collective-permute-start
  13.2 1.0 reduce-window.9
  14.5 0.8 fusion.23
  15.3 0.7 convert_element_type.87
  16.0 1.4 copy.17
  17.4 1.5 pad_maximum_fusion
  19.1 1.0 copy-done.3
  20.0 0.7 fusion.11
  21.5 7.5 %fusion.2 = bf16[4096,128]{1,0:T(8,128)(2,1)} fusion(f32[4096]{0:T(1024)S(1)} %convert_element_type.87, s32[1024]{0:T(1024)S(1)} %add_multiply_fusion, s32[4096]{0:T(1024)S(1)} %get-tuple-element.4, s32[1024]{0:T(1024)S(1)} %broadcast_add_fusion, s32[4096]{0:T(1024)S(1)} %get-tuple-element.5, bf16[1,128,1024]{1,2,0:T(8,128)(2,1)S(1)} %fusion.11), kind=kOutput, calls=%fused_computation.3 | convolution fusion | flops 1103626240 | bytes 1368064 | tf_op jit(solution)/shard_map/dot_general | solution.py:51
  29.1 38.1 %reduce-scatter.5.cloned.1.call-done = bf16[1024,128]{1,0:T(8,128)(2,1)} async-done(((bf16[4096,128]{1,0:T(8,128)(2,1)}), bf16[1024,128]{1,0:T(8,128)(2,1)}) %reduce-scatter.5.cloned.1.call-update) | async-done | bytes 262160 | tf_op jit(solution)/shard_map/reduce_scatter | solution.py:50
  67.3 80.8 %all-gather.3.cloned.1.call-done = bf16[1024,2048]{1,0:T(8,128)(2,1)} async-done(((bf16[1024,128]{1,0:T(8,128)(2,1)}), bf16[1024,2048]{1,0:T(8,128)(2,1)}) %all-gather.3.cloned.1.call-update) | async-done | bytes 4194320 | tf_op jit(solution)/shard_map/all_gather | solution.py:56
  148.1 4.6 fusion.24
  152.7 1.4 copy-done.9
  154.0 4.4 convert_bitcast_fusion
  158.4 6.4 %copy.23 = bf16[2048,1024]{1,0:T(8,128)(2,1)} copy(bf16[2048,1024]{0,1:T(8,128)(2,1)} %convert_bitcast_fusion) | data formatting | bytes 8388608
  164.9 78.5 %reduce-scatter.7.cloned.1.call-done = bf16[128,1024]{1,0:T(8,128)(2,1)} async-done(((bf16[2048,1024]{1,0:T(8,128)(2,1)}), bf16[128,1024]{1,0:T(8,128)(2,1)}) %reduce-scatter.7.cloned.1.call-update) | async-done | bytes 262160
  243.4 1.8 copy.24
  245.3 6.8 %convolution_convert_fusion = bf16[2048,512]{1,0:T(8,128)(2,1)} fusion(bf16[1024,2048]{1,0:T(8,128)(2,1)} %all-gather.3.cloned.1.call-done, f32[1024,512]{1,0:T(8,128)} %copy-done.9, bf16[1,1024,512]{2,1,0:T(8,128)(2,1)} %param.10), kind=kOutput, calls=%fused_computation.6 | convolution fusion | flops 2150105088 | bytes 9437184 | tf_op jit(solution)/shard_map/dot_general | solution.py:59
  252.3 24.6 %all-gather.5.cloned.1.call-done = bf16[128,4096]{0,1:T(8,128)(2,1)} async-done(((bf16[128,1024]{0,1:T(8,128)(2,1)}), bf16[128,4096]{0,1:T(8,128)(2,1)}) %all-gather.5.cloned.1.call-update) | async-done | bytes 1048592 | tf_op jit(solution)/shard_map/all_gather | solution.py:77
  276.9 7.6 %fusion.15 = bf16[1024,128,1]{1,0,2:T(8,128)(2,1)S(1)} fusion(bf16[128,4096]{0,1:T(8,128)(2,1)} %all-gather.5.cloned.1.call-done, f32[4096]{0:T(1024)S(1)} %convert_element_type.87, s32[1024]{0:T(1024)S(1)} %add_multiply_fusion, s32[4096]{0:T(1024)S(1)} %get-tuple-element.4, s32[1024]{0:T(1024)S(1)} %broadcast_add_fusion, s32[4096]{0:T(1024)S(1)} %get-tuple-element.5), kind=kOutput, calls=%fused_computation.21 | convolution fusion | flops 1103233024 | bytes 1368064 | tf_op jit(solution)/shard_map/dot_general | solution.py:75
  285.2 1.9 copy-done.1
  287.2 2.1 collective-permute-start.1
  289.2 1.5 fusion.14
  290.8 137.6 %all-reduce.8.cloned.1.call-done = bf16[2048,512]{1,0:T(8,128)(2,1)} async-done(((bf16[2048,512]{1,0:T(8,128)(2,1)}), bf16[2048,512]{1,0:T(8,128)(2,1)}) %all-reduce.8.cloned.1.call-update) | async-done | bytes 2097168 | tf_op jit(solution)/shard_map/psum | solution.py:63
  428.4 4.3 convert_multiply_fusion
  432.8 1.5 slice.46
  434.2 45.1 %all-reduce.4.cloned.1.call-done = bf16[1,8,128,128]{3,2,1,0:T(8,128)(2,1)} async-done(((bf16[1,8,128,128]{3,2,1,0:T(8,128)(2,1)}), bf16[1,8,128,128]{3,2,1,0:T(8,128)(2,1)}) %all-reduce.4.cloned.1.call-update) | async-done | bytes 262160 | tf_op jit(solution)/shard_map/psum | solution.py:85
  479.4 2.5 fusion.3
  481.9 1.8 copy.20
  483.7 41.6 %all-reduce.6.cloned.1.call-done = bf16[1,8,128,128]{3,2,1,0:T(8,128)(2,1)} async-done(((bf16[1,8,128,128]{3,2,1,0:T(8,128)(2,1)}), bf16[1,8,128,128]{3,2,1,0:T(8,128)(2,1)}) %all-reduce.6.cloned.1.call-update) | async-done | bytes 262160 | tf_op jit(solution)/shard_map/psum | solution.py:85
  525.3 1.8 convert_multiply_fusion.1
  (41 shorter events, 2.4 us)
Async XLA Ops:
  7.2 140.9 %copy-start = (bf16[2048,512]{1,0:T(8,128)(2,1)S(1)}, bf16[2048,512]{1,0:T(8,128)(2,1)}, u32[]{:S(2)}) copy-start(bf16[2048,512]{1,0:T(8,128)(2,1)} %param.9) | copy-start | bytes 6291460
  7.2 12.9 %copy-start.7 = (f32[128]{0:T(128)S(1)}, f32[128]{0:T(128)}, u32[]{:S(2)}) copy-start(f32[128]{0:T(128)} %param.8) | copy-start | bytes 1540
  7.2 12.8 %copy-start.5 = (bf16[1,1024,128]{2,1,0:T(8,128)(2,1)S(1)}, bf16[1,1024,128]{2,1,0:T(8,128)(2,1)}, u32[]{:S(2)}) copy-start(bf16[1,1024,128]{2,1,0:T(8,128)(2,1)} %param.7) | copy-start | bytes 786436
  7.2 60.0 %reduce-scatter.5.cloned.1.call-start = ((), (), s32[]{:S(2)}) async-start(), calls=%async_computation.2 | async-start | bytes 1310720 | tf_op jit(solution)/shard_map/reduce_scatter | solution.py:50
  8.1 9.3 %collective-permute-start = (bf16[4,128]{1,0:T(4,128)(2,1)S(1)}, bf16[4,128]{1,0:T(4,128)(2,1)S(1)}, u32[]{:S(2)}, u32[]{:S(2)}) collective-permute-start(bf16[4,128]{1,0:T(4,128)(2,1)S(1)} %slice_bitcast_fusion), channel_id=1, source_target_pairs={{16,0},{32,16},{48,32},{17,1},{33,17},{49,33},{18,2},{34,18},{50,3... | collective-permute-start | bytes 3080 | tf_op jit(solution)/shard_map/ppermute | solution.py:13
  19.0 1.0 copy-start.3
  20.8 0.7 copy-start.8
  29.0 119.1 %all-gather.3.cloned.1.call-start = ((), (), s32[]{:S(2)}) async-start(), calls=%async_computation.3 | async-start | bytes 4456448 | tf_op jit(solution)/shard_map/all_gather | solution.py:56
  67.2 176.2 %reduce-scatter.7.cloned.1.call-start = ((), (), s32[]{:S(2)}) async-start(), calls=%async_computation.8 | async-start | bytes 4456448
  148.1 6.0 %copy-start.6 = (bf16[1,1024,512]{2,1,0:T(8,128)(2,1)S(1)}, bf16[1,1024,512]{2,1,0:T(8,128)(2,1)}, u32[]{:S(2)}) copy-start(bf16[1,1024,512]{2,1,0:T(8,128)(2,1)} %param.10) | copy-start | bytes 3145732
  152.7 1.4 copy-start.9
  164.9 112.0 %all-gather.5.cloned.1.call-start = ((), (), s32[]{:S(2)}) async-start(), calls=%async_computation.4 | async-start | bytes 1310720 | tf_op jit(solution)/shard_map/all_gather | solution.py:77
  245.2 183.2 %all-reduce.8.cloned.1.call-start = ((), (), s32[]{:S(2)}) async-start(), calls=%async_computation.7 | async-start | bytes 4194304 | tf_op jit(solution)/shard_map/psum | solution.py:63
  252.1 227.3 %all-reduce.4.cloned.1.call-start = ((), (), s32[]{:S(2)}) async-start(), calls=%async_computation.5 | async-start | bytes 524288 | tf_op jit(solution)/shard_map/psum | solution.py:85
  284.5 4.7 copy-start.4
  285.2 1.9 copy-start.1
  287.2 192.2 %collective-permute-start.1 = (f32[4,1,128]{2,0,1:T(4,128)S(1)}, f32[4,1,128]{2,0,1:T(4,128)S(1)}, u32[]{:S(2)}, u32[]{:S(2)}) collective-permute-start(f32[4,1,128]{2,0,1:T(4,128)S(1)} %bitcast.91), channel_id=1, source_target_pairs={{0,16},{16,32},{32,48},{1,17},{17,33},{33,49},{2,18},{18,34},{34,5... | collective-permute-start | bytes 6152 | tf_op jit(solution)/shard_map/ppermute | solution.py:13
  290.7 234.6 %all-reduce.6.cloned.1.call-start = ((), (), s32[]{:S(2)}) async-start(), calls=%async_computation.6 | async-start | bytes 524288 | tf_op jit(solution)/shard_map/psum | solution.py:85
  428.4 4.4 copy-start.2
Sparse Core Ops, SparseCore 0:
  29.1 38.0 reduce-scatter.4
  69.0 79.0 all-gather.2
  165.0 78.3 reduce-scatter.6
  245.8 31.0 all-gather.4
  280.2 148.2 all-reduce.7
  431.7 47.6 all-reduce.3
  481.7 43.5 all-reduce.5
